TPU v7x, 32 devices: a whole 2x2x4 slice. The times are simulated.
32 devices in a mesh: groups: 2 (over y), area: 4 (over z), neuron: 4 (over x, core).
Axes of the slice: x: 2, y: 2, z: 4, core: 2. Of those that a mesh axis runs over, the one named last changes fastest.
Arguments:
- window: bfloat16 [32, 16, 32768], P(None, 'groups', ('area', 'neuron')), parts along dimension 1, may hold values from -6 to 6
- err_grad: float32 [16, 16, 32768], P(None, 'groups', ('area', 'neuron')), parts along dimension 1, may hold values from -6 to 6
- surrogate: float32 [16, 16, 32768], P(None, 'groups', ('area', 'neuron')), parts along dimension 1, may hold values from 0 to 0.5
- lv_end: float32 [16, 32768], P('groups', ('area', 'neuron')), parts along dimension 0, may hold values from -6 to 6
- la_end: float32 [16, 32768], P('groups', ('area', 'neuron')), parts along dimension 0, may hold values from -6 to 6
- alpha: float32 [32768], P(('area', 'neuron')), may hold values from 0.8 to 0.99
- rho: float32 [32768], P(('area', 'neuron')), may hold values from 0.9 to 0.999
- beta: float32 [32768], P(('area', 'neuron')), may hold values from 0.3 to 2
- weights: bfloat16 [4, 4, 64, 4, 128, 128], P(None, 'area', 'neuron'), may hold values from -0.25 to 0.25
- block_index: int32 [4, 4, 64, 4], P(None, 'area', 'neuron'), may hold values from 0 to 63, as said below
- delays: int32 [4, 4], replicated, may hold values from 16 to 31, as said below
Outputs:
- cur_adjoint: bfloat16 [16, 16, 32768], P(None, 'groups', ('area', 'neuron')), parts along dimension 1
- lv_start: float32 [16, 32768], P('groups', ('area', 'neuron')), parts along dimension 0
- la_start: float32 [16, 32768], P('groups', ('area', 'neuron')), parts along dimension 0
There are 2 independent parts, one for each index of `groups`. A program takes and returns all parts, laid end to end along the dimension named above; an argument that names none is the same for every part. Nothing has to cross between parts.
Inputs may be any that keep to these rules, and one draw needn't show every extreme that they name: `delays`: every entry lies in 16 to 31 and both ends occur. `block_index`: both ends occur.
All inputs are finite; a program needn't handle non-finite values.
Results may differ from a plain program's by a relative error of at most 0.001.
Values may be sent and summed in bfloat16 or wider, within the bound.
No kernel may reach another device: no remote copies, remote signals or barrier semaphores. Data moves between devices by JAX's collectives and lax.ppermute only.
A program may use at most 64 MiB of HBM per device.

v0:
```python
import jax
import jax.numpy as jnp
from jax import lax
from jax.sharding import PartitionSpec as P


def partner(value, axis, bit):
    mask = 2**bit
    pairs = [(source, source ^ mask) for source in range(lax.axis_size(axis))]
    return lax.ppermute(value, axis, pairs)


def adjoint_scan(err_grad, surrogate, rec, lv_end, la_end, alpha, rho, beta):

    def step(carry, inputs):
        lv_now, la_now = carry
        error_t, surr_t, rec_t = inputs
        total = error_t + rec_t - lv_now + la_now
        lv_next = alpha * lv_now + surr_t * total
        la_next = rho * la_now - beta * surr_t * total
        return ((lv_next, la_next), lv_now.astype(jnp.bfloat16))

    (lv_start, la_start), currents = lax.scan(
        step, (lv_end, la_end), (err_grad, surrogate, rec), reverse=True
    )
    return (currents, lv_start, la_start)


def per_device(
    window, err_grad, surrogate, lv_end, la_end, alpha, rho, beta, weights, block_index, delays
):
    steps = err_grad.shape[0]
    batch = err_grad.shape[1]
    local_neurons = err_grad.shape[2]
    block_side = weights.shape[-1]
    rounds = weights.shape[0]
    levels = lax.axis_size("area").bit_length() - 1
    me_area = lax.axis_index("area")
    rec = jnp.zeros((steps * batch, local_neurons), jnp.float32)
    for rnd in range(rounds):
        bit = rnd % levels
        arrived = partner(window, "area", bit)
        start = delays[rnd, me_area] - steps
        used = lax.dynamic_slice_in_dim(arrived, start, steps, 0)
        panel = lax.all_gather(used, "neuron", axis=2, tiled=True)
        flat = panel.reshape(steps * batch, panel.shape[2] // block_side, block_side)
        picked = jnp.take(flat, block_index[rnd, 0], axis=1)
        contrib = jnp.einsum(
            "rjkc,jkcd->rjd", picked, weights[rnd, 0], preferred_element_type=jnp.float32
        )
        rec = rec + contrib.reshape(steps * batch, local_neurons)
    rec = rec.reshape(steps, batch, local_neurons)
    return adjoint_scan(err_grad, surrogate, rec, lv_end, la_end, alpha, rho, beta)


def solution(mesh):
    placed = (
        P(None, "groups", ("area", "neuron")),
        P(None, "groups", ("area", "neuron")),
        P(None, "groups", ("area", "neuron")),
        P("groups", ("area", "neuron")),
        P("groups", ("area", "neuron")),
        P(("area", "neuron")),
        P(("area", "neuron")),
        P(("area", "neuron")),
        P(None, "area", "neuron", None, None, None),
        P(None, "area", "neuron", None),
        P(),
    )
    return jax.shard_map(
        per_device,
        mesh=mesh,
        in_specs=placed,
        out_specs=(
            P(None, "groups", ("area", "neuron")),
            P("groups", ("area", "neuron")),
            P("groups", ("area", "neuron")),
        ),
        check_vma=False,
    )
```

profile of v0, /device:TPU:0, one launch (start us, length us, event | category | flops | bytes accessed | tf_op | source)
XLA Modules:
  0.0 206.2 jit_solution(3993261804340114842)
XLA Ops:
  7.2 3.1 %collective-permute-start = (bf16[32,8,2048]{2,1,0:T(8,128)(2,1)}, bf16[32,8,2048]{2,1,0:T(8,128)(2,1)S(1)}, u32[]{:S(2)}, u32[]{:S(2)}) collective-permute-start(bf16[32,8,2048]{2,1,0:T(8,128)(2,1)} %param.15), channel_id=1, source_target_pairs={{0,4},{4,0},{8,12},{12,8},{1,5},{5,1},{9,13},{13,9},{2,6},{6,2},{1... | collective-permute-start | bytes 3145736 | tf_op jit(solution)/shard_map/ppermute | solution.py:10
  10.3 1.5 constant_dynamic-slice_fusion.5
  14.4 19.3 %collective-permute-done = bf16[32,8,2048]{2,1,0:T(8,128)(2,1)S(1)} collective-permute-done((bf16[32,8,2048]{2,1,0:T(8,128)(2,1)}, bf16[32,8,2048]{2,1,0:T(8,128)(2,1)S(1)}, u32[]{:S(2)}, u32[]{:S(2)}) %collective-permute-start) | collective-permute-done | bytes 1048608 | tf_op jit(solution)/shard_map/ppermute | solution.py:10
  34.9 2.8 %collective-permute-start.1 = (bf16[32,8,2048]{2,1,0:T(8,128)(2,1)S(1)}, bf16[32,8,2048]{2,1,0:T(8,128)(2,1)S(1)}, u32[]{:S(2)}, u32[]{:S(2)}) collective-permute-start(bf16[32,8,2048]{2,1,0:T(8,128)(2,1)S(1)} %copy-done.12), channel_id=1, source_target_pairs={{0,8},{4,12},{8,0},{12,4},{1,9},{5,13},{9,1},{13,5},{2,10},{6,14},... | collective-permute-start | bytes 3145736 | tf_op jit(solution)/shard_map/ppermute | solution.py:10
  40.1 42.5 %collective-permute-done.1 = bf16[32,8,2048]{2,1,0:T(8,128)(2,1)S(1)} collective-permute-done((bf16[32,8,2048]{2,1,0:T(8,128)(2,1)S(1)}, bf16[32,8,2048]{2,1,0:T(8,128)(2,1)S(1)}, u32[]{:S(2)}, u32[]{:S(2)}) %collective-permute-start.1) | collective-permute-done | bytes 1048608 | tf_op jit(solution)/shard_map/ppermute | solution.py:10
  86.2 2.2 %copy.52 = bf16[16,8,64,128]{3,2,1,0:T(8,128)(2,1)S(1)} copy(bf16[16,8,64,128]{3,1,2,0:T(8,128)(2,1)} %bitcast.147) | data formatting | bytes 4194304
  89.8 17.6 %all-gather.7.cloned.1.call-done = bf16[16,8,8192]{2,1,0:T(8,128)(2,1)} async-done(((bf16[16,8,2048]{2,1,0:T(8,128)(2,1)}), bf16[16,8,8192]{2,1,0:T(8,128)(2,1)}) %all-gather.7.cloned.1.call-update) | async-done | bytes 2097168 | tf_op jit(solution)/shard_map/all_gather | solution.py:45
  107.4 2.2 %copy.53 = bf16[16,8,64,128]{3,2,1,0:T(8,128)(2,1)S(1)} copy(bf16[16,8,64,128]{3,1,2,0:T(8,128)(2,1)} %bitcast.148) | data formatting | bytes 4194304
  109.6 2.7 %copy.40 = bf16[128,64,128]{2,0,1:T(8,128)(2,1)} copy(bf16[128,64,128]{2,1,0:T(8,128)(2,1)S(1)} %bitcast.144) | data formatting | bytes 4194304 | tf_op jit(solution)/shard_map/reshape | solution.py:46
  112.3 19.9 %all-gather.9.cloned.1.call-done = bf16[16,8,8192]{2,1,0:T(8,128)(2,1)} async-done(((bf16[16,8,2048]{2,1,0:T(8,128)(2,1)}), bf16[16,8,8192]{2,1,0:T(8,128)(2,1)}) %all-gather.9.cloned.1.call-update) | async-done | bytes 2097168 | tf_op jit(solution)/shard_map/all_gather | solution.py:45
  132.2 2.2 %copy.54 = bf16[16,8,64,128]{3,2,1,0:T(8,128)(2,1)S(1)} copy(bf16[16,8,64,128]{3,1,2,0:T(8,128)(2,1)} %bitcast.149) | data formatting | bytes 4194304
  134.4 2.7 %copy.43 = bf16[128,64,128]{2,0,1:T(8,128)(2,1)} copy(bf16[128,64,128]{2,1,0:T(8,128)(2,1)S(1)} %bitcast.145) | data formatting | bytes 4194304 | tf_op jit(solution)/shard_map/reshape | solution.py:46
  137.1 19.1 %all-gather.11.cloned.1.call-done = bf16[16,8,8192]{2,1,0:T(8,128)(2,1)} async-done(((bf16[16,8,2048]{2,1,0:T(8,128)(2,1)}), bf16[16,8,8192]{2,1,0:T(8,128)(2,1)}) %all-gather.11.cloned.1.call-update) | async-done | bytes 2097168 | tf_op jit(solution)/shard_map/all_gather | solution.py:45
  156.2 2.2 %copy.55 = bf16[16,8,64,128]{3,2,1,0:T(8,128)(2,1)S(1)} copy(bf16[16,8,64,128]{3,1,2,0:T(8,128)(2,1)} %bitcast.150) | data formatting | bytes 4194304
  158.4 2.7 %copy.46 = bf16[128,64,128]{2,0,1:T(8,128)(2,1)} copy(bf16[128,64,128]{2,1,0:T(8,128)(2,1)S(1)} %bitcast.146) | data formatting | bytes 4194304 | tf_op jit(solution)/shard_map/reshape | solution.py:46
  161.1 2.1 %gather_fusion = bf16[64,128,128]{2,1,0:T(8,128)(2,1)} fusion(bf16[128,64,128]{2,0,1:T(8,128)(2,1)S(1)} %copy.37, s32[1024]{0:T(1024)S(1)} %pad_clamp_fusion.3), kind=kCustom, calls=%fused_computation.clone | custom fusion | bytes 4194560 | tf_op jit(solution)/shard_map/jit(_take)/gather | solution.py:47
  163.3 4.0 %gather_fusion.1 = bf16[64,128,128]{2,1,0:T(8,128)(2,1)} fusion(bf16[128,64,128]{2,0,1:T(8,128)(2,1)} %copy.40, s32[1024]{0:T(1024)S(1)} %pad_clamp_fusion.2), kind=kCustom, calls=%fused_computation.1.clone | custom fusion | bytes 4194560 | tf_op jit(solution)/shard_map/jit(_take)/gather | solution.py:47
  167.2 2.2 %gather_fusion.2 = bf16[64,128,128]{2,1,0:T(8,128)(2,1)} fusion(bf16[128,64,128]{2,0,1:T(8,128)(2,1)S(1)} %copy-done, s32[1024]{0:T(1024)S(1)} %pad_clamp_fusion.1), kind=kCustom, calls=%fused_computation.2.clone | custom fusion | bytes 4194560 | tf_op jit(solution)/shard_map/jit(_take)/gather | solution.py:47
  169.4 2.5 %gather_fusion.3 = bf16[64,128,128]{2,1,0:T(8,128)(2,1)S(1)} fusion(bf16[128,64,128]{2,0,1:T(8,128)(2,1)} %copy.46, s32[1024]{0:T(1024)S(1)} %pad_clamp_fusion), kind=kCustom, calls=%fused_computation.3.clone | custom fusion | bytes 4194560 | tf_op jit(solution)/shard_map/jit(_take)/gather | solution.py:47
  172.0 3.1 %fusion.28 = f32[16,128,128]{2,1,0:T(8,128)S(1)} fusion(bf16[4,1,16,4,128,128]{5,4,3,2,1,0:T(8,128)(2,1)} %param.23, bf16[16,4,128,128]{3,2,1,0:T(8,128)(2,1)} %bitcast.153, pred[16,4]{1,0:T(8,128)(4,1)S(1)} %copy.35), kind=kOutput, calls=%fused_computation.36 | convolution fusion | flops 269484032 | bytes 5242944 | tf_op jit(solution)/shard_map/rjkc,jkcd->rjd/dot_general | solution.py:48
  175.1 2.5 %fusion.63 = f32[16,128,128]{2,1,0:T(8,128)S(1)} fusion(f32[16,128,128]{2,1,0:T(8,128)S(1)} %fusion.28, bf16[4,1,16,4,128,128]{5,4,3,2,1,0:T(8,128)(2,1)} %param.23, bf16[16,4,128,128]{3,2,1,0:T(8,128)(2,1)S(1)} %bitcast.154, pred[16,4]{1,0:T(8,128)(4,1)S(1)} %copy.38), kind=kOutput, calls=%fused_computation.43 | convolution fusion | flops 269746176 | bytes 6291520 | tf_op jit(solution)/shard_map/rjkc,jkcd->rjd/dot_general | solution.py:48
  177.6 2.4 %fusion.58 = f32[16,128,128]{2,1,0:T(8,128)S(1)} fusion(f32[16,128,128]{2,1,0:T(8,128)S(1)} %fusion.63, bf16[4,1,16,4,128,128]{5,4,3,2,1,0:T(8,128)(2,1)} %param.23, bf16[16,4,128,128]{3,2,1,0:T(8,128)(2,1)S(1)} %bitcast.152, pred[16,4]{1,0:T(8,128)(4,1)S(1)} %copy.41), kind=kOutput, calls=%fused_computation.42 | convolution fusion | flops 269746176 | bytes 6291520 | tf_op jit(solution)/shard_map/rjkc,jkcd->rjd/dot_general | solution.py:48
  180.0 2.4 %fusion.53 = f32[128,16,128]{2,0,1:T(8,128)S(1)} fusion(f32[16,128,128]{2,1,0:T(8,128)S(1)} %fusion.58, bf16[4,1,16,4,128,128]{5,4,3,2,1,0:T(8,128)(2,1)} %param.23, bf16[16,4,128,128]{3,2,1,0:T(8,128)(2,1)S(1)} %bitcast.151, pred[16,4]{1,0:T(8,128)(4,1)S(1)} %copy.44), kind=kOutput, calls=%fused_computation.41 | convolution fusion | flops 269746176 | bytes 6291520 | tf_op jit(solution)/shard_map/rjkc,jkcd->rjd/dot_general | solution.py:48
  183.4 15.5 %while.18 = (s32[]{:T(128)}, f32[8,2048]{1,0:T(8,128)S(1)}, f32[8,2048]{1,0:T(8,128)S(1)}, bf16[16,8,2048]{2,1,0:T(8,128)(2,1)S(1)}, f32[2048]{0:T(1024)S(1)}, /...) while((s32[]{:T(128)}, f32[8,2048]{1,0:T(8,128)S(1)}, ...), condition=%wide.region_1.3_spmd, body=%wide.region_0.0_spmd.sunk | while | flops 180227 | bytes 581769 | solution.py:23
  (91 shorter events, 22.8 us)
Async XLA Ops:
  7.2 27.7 %copy-start.12 = (bf16[32,8,2048]{2,1,0:T(8,128)(2,1)S(1)}, bf16[32,8,2048]{2,1,0:T(8,128)(2,1)}, u32[]{:S(2)}) copy-start(bf16[32,8,2048]{2,1,0:T(8,128)(2,1)} %param.15) | copy-start | bytes 3145732
  7.2 79.0 %all-gather.5.cloned.1.call-start = ((), (), s32[]{:S(2)}) async-start(), calls=%async_computation | async-start | bytes 2621440 | tf_op jit(solution)/shard_map/all_gather | solution.py:45
  7.2 26.5 %collective-permute-start = (bf16[32,8,2048]{2,1,0:T(8,128)(2,1)}, bf16[32,8,2048]{2,1,0:T(8,128)(2,1)S(1)}, u32[]{:S(2)}, u32[]{:S(2)}) collective-permute-start(bf16[32,8,2048]{2,1,0:T(8,128)(2,1)} %param.15), channel_id=1, source_target_pairs={{0,4},{4,0},{8,12},{12,8},{1,5},{5,1},{9,13},{13,9},{2,6},{6,2},{1... | collective-permute-start | bytes 3145736 | tf_op jit(solution)/shard_map/ppermute | solution.py:10
  34.8 50.2 %copy-start.11 = (s32[4,1,16,4]{2,3,1,0:T(4,128)S(1)}, s32[4,1,16,4]{2,3,1,0:T(4,128)}, u32[]{:S(2)}) copy-start(s32[4,1,16,4]{2,3,1,0:T(4,128)} %param.24) | copy-start | bytes 3076
  34.8 72.6 %all-gather.7.cloned.1.call-start = ((), (), s32[]{:S(2)}) async-start(), calls=%async_computation.1 | async-start | bytes 2621440 | tf_op jit(solution)/shard_map/all_gather | solution.py:45
  34.9 47.8 %collective-permute-start.1 = (bf16[32,8,2048]{2,1,0:T(8,128)(2,1)S(1)}, bf16[32,8,2048]{2,1,0:T(8,128)(2,1)S(1)}, u32[]{:S(2)}, u32[]{:S(2)}) collective-permute-start(bf16[32,8,2048]{2,1,0:T(8,128)(2,1)S(1)} %copy-done.12), channel_id=1, source_target_pairs={{0,8},{4,12},{8,0},{12,4},{1,9},{5,13},{9,1},{13,5},{2,10},{6,14},... | collective-permute-start | bytes 3145736 | tf_op jit(solution)/shard_map/ppermute | solution.py:10
  83.7 48.5 %all-gather.9.cloned.1.call-start = ((), (), s32[]{:S(2)}) async-start(), calls=%async_computation.2 | async-start | bytes 2621440 | tf_op jit(solution)/shard_map/all_gather | solution.py:45
  84.4 71.8 %all-gather.11.cloned.1.call-start = ((), (), s32[]{:S(2)}) async-start(), calls=%async_computation.3 | async-start | bytes 2621440 | tf_op jit(solution)/shard_map/all_gather | solution.py:45
  163.3 4.0 %copy-start = (bf16[128,64,128]{2,0,1:T(8,128)(2,1)S(1)}, bf16[128,64,128]{2,0,1:T(8,128)(2,1)}, u32[]{:S(2)}) copy-start(bf16[128,64,128]{2,0,1:T(8,128)(2,1)} %copy.43) | copy-start | bytes 6291460
  171.9 3.1 %copy-start.6 = (bf16[64,128,128]{2,1,0:T(8,128)(2,1)S(1)}, bf16[64,128,128]{2,1,0:T(8,128)(2,1)}, u32[]{:S(2)}) copy-start(bf16[64,128,128]{2,1,0:T(8,128)(2,1)} %gather_fusion.1) | copy-start | bytes 6291460
  175.1 2.6 %copy-start.5 = (bf16[64,128,128]{2,1,0:T(8,128)(2,1)S(1)}, bf16[64,128,128]{2,1,0:T(8,128)(2,1)}, u32[]{:S(2)}) copy-start(bf16[64,128,128]{2,1,0:T(8,128)(2,1)} %gather_fusion.2) | copy-start | bytes 6291460
  182.4 0.9 copy-start.2
  182.5 0.9 copy-start.4
  182.5 0.9 copy-start.8
  182.5 0.9 copy-start.9
  182.5 0.9 copy-start.10
  198.8 0.6 copy-start.1
  198.9 0.6 copy-start.3
  198.9 0.8 copy-start.7
Sparse Core Ops, SparseCore 0:
  34.9 23.9 all-gather.4
  83.8 23.5 all-gather.6
  109.6 22.5 all-gather.8
  133.6 22.5 all-gather.10
where the time goes:
time: 207 us; the launch traced here: 206 us
  waiting for transfers between devices  120 us (58%)
  local copies, waits for them, and re-layouts  35.4 us (17%)
  between operations  19.1 us (9%)
  other arithmetic  15.2 us (7%)
  matrix products  10.4 us (5%)
  starting transfers between devices  6.07 us (3%)
    ppermute x2, waiting for transfers between devices, partner(): return lax.ppermute(value, axis, pairs)  61.8 us
    all_gather x4, waiting for transfers between devices, per_device(): panel = lax.all_gather(used, 'neuron', axis=2, tiled=True)  56.6 us
    sub x16, other arithmetic, step(): la_next = rho * la_now - beta * surr_t * total  15 us
    gather x4, local copies, waits for them, and re-layouts, per_device(): picked = jnp.take(flat, block_index[rnd, 0], axis=1)  10.8 us
    dot_general x4, matrix products, per_device(): jnp.einsum('rjkc,jkcd->rjd', picked, weights[rnd, 0], preferred_element_t...  10.4 us
    unnamed x30, local copies, waits for them, and re-layouts  9.6 us
    reshape x4, local copies, waits for them, and re-layouts, per_device(): panel.reshape(steps * batch, panel.shape[2] // block_side, block_side)  9.53 us
    ppermute x2, starting transfers between devices, partner(): return lax.ppermute(value, axis, pairs)  5.91 us
  transfers between devices with their start and end apart: 6, of which 5 were waited for; matrix products, arithmetic and copies ran while one was open for 8% of the time, Pallas kernels for 0%

commit v1 on v0

--- a/solution.py
+++ b/solution.py
@@ -2,6 +2,23 @@
 import jax.numpy as jnp
 from jax import lax
 from jax.sharding import PartitionSpec as P
+
+
+def in_order(blocks, dim):
+    shape = list(blocks.shape[1:])
+    shape[dim] *= blocks.shape[0]
+    return jnp.moveaxis(blocks, 0, dim).reshape(shape)
+
+
+def grow_blocks(x, axis):
+    count, position = (lax.axis_size(axis), lax.axis_index(axis))
+    pieces, bit = (x[None], 1)
+    while bit < count:
+        theirs = lax.ppermute(pieces, axis, [(i, i ^ bit) for i in range(count)])
+        low = position & bit == 0
+        pieces = jnp.concatenate([jnp.where(low, pieces, theirs), jnp.where(low, theirs, pieces)])
+        bit *= 2
+    return pieces
 
 
 def partner(value, axis, bit):
@@ -42,7 +59,7 @@
         arrived = partner(window, "area", bit)
         start = delays[rnd, me_area] - steps
         used = lax.dynamic_slice_in_dim(arrived, start, steps, 0)
-        panel = lax.all_gather(used, "neuron", axis=2, tiled=True)
+        panel = in_order(grow_blocks(used, "neuron"), 2)
         flat = panel.reshape(steps * batch, panel.shape[2] // block_side, block_side)
         picked = jnp.take(flat, block_index[rnd, 0], axis=1)
         contrib = jnp.einsum(

time: 207 us -> 217 us (1.048)
  local copies, waits for them, and re-layouts: 35.4 us -> 60.7 us
  waiting for transfers between devices: 120 us -> 102 us
  between operations: 19.1 us -> 6.08 us
  other arithmetic: 15.2 us -> 24.9 us
  starting transfers between devices: 6.07 us -> 11.3 us
    ppermute x0 -> x8, waiting for transfers between devices: none -> 63.2 us  [grow_blocks(): theirs = lax.ppermute(pieces, axis, [(i, i ^ bit) for i in range(count)])]
    all_gather x4 -> x0, waiting for transfers between devices: 56.6 us -> none  [per_device(): panel = lax.all_gather(used, 'neuron', axis=2, tiled=True)]
    another operation x0 -> x8, local copies, waits for them, and re-layouts: none -> 32.3 us  [per_device(): panel.reshape(steps * batch, panel.shape[2] // block_side, block_side)]
    ppermute x2, waiting for transfers between devices: 61.8 us -> 38.5 us  [partner(): return lax.ppermute(value, axis, pairs)]
    transpose x0 -> x4, local copies, waits for them, and re-layouts: none -> 11.1 us  [in_order(): return jnp.moveaxis(blocks, 0, dim).reshape(shape)]
    reshape x4 -> x0, local copies, waits for them, and re-layouts: 9.53 us -> none  [per_device(): panel.reshape(steps * batch, panel.shape[2] // block_side, block_side)]
    unnamed x30 -> x38, local copies, waits for them, and re-layouts: 9.6 us -> 1.7 us
    ppermute x0 -> x8, starting transfers between devices: none -> 5.62 us  [grow_blocks(): theirs = lax.ppermute(pieces, axis, [(i, i ^ bit) for i in range(count)])]
  transfers between devices with their start and end apart: 6 -> 10, of which waited for: 5 -> 5; matrix products, arithmetic and copies ran while one was open for 8% -> 14% of each run, Pallas kernels for 0% -> 0%
where the time goes in v1:
time: 217 us; the launch traced here: 216 us
  waiting for transfers between devices  102 us (47%)
  local copies, waits for them, and re-layouts  60.7 us (28%)
  other arithmetic  24.9 us (11%)
  starting transfers between devices  11.3 us (5%)
  matrix products  10.4 us (5%)
  between operations  6.08 us (3%)
    ppermute x8, waiting for transfers between devices, grow_blocks(): theirs = lax.ppermute(pieces, axis, [(i, i ^ bit) for i in range(count)])  63.2 us
    ppermute x2, waiting for transfers between devices, partner(): return lax.ppermute(value, axis, pairs)  38.5 us
    another operation x8, local copies, waits for them, and re-layouts, per_device(): panel.reshape(steps * batch, panel.shape[2] // block_side, block_side)  32.3 us
    sub x16, other arithmetic, step(): la_next = rho * la_now - beta * surr_t * total  15 us
    transpose x4, local copies, waits for them, and re-layouts, in_order(): return jnp.moveaxis(blocks, 0, dim).reshape(shape)  11.1 us
    gather x4, local copies, waits for them, and re-layouts, per_device(): picked = jnp.take(flat, block_index[rnd, 0], axis=1)  10.9 us
    dot_general x4, matrix products, per_device(): jnp.einsum('rjkc,jkcd->rjd', picked, weights[rnd, 0], preferred_element_t...  10.4 us
    ppermute x2, starting transfers between devices, partner(): return lax.ppermute(value, axis, pairs)  5.68 us
  transfers between devices with their start and end apart: 10, of which 5 were waited for; matrix products, arithmetic and copies ran while one was open for 14% of the time, Pallas kernels for 0%

profile of v1, /device:TPU:0, one launch (start us, length us, event | category | flops | bytes accessed | tf_op | source)
XLA Modules:
  0.0 215.5 jit_solution(8594273243336271734)
XLA Ops:
  0.6 4.1 %collective-permute-start.3 = (bf16[32,8,2048]{2,1,0:T(8,128)(2,1)}, bf16[32,8,2048]{2,1,0:T(8,128)(2,1)}, u32[]{:S(2)}, u32[]{:S(2)}) collective-permute-start(bf16[32,8,2048]{2,1,0:T(8,128)(2,1)} %param.15), channel_id=1, source_target_pairs={{0,8},{4,12},{8,0},{12,4},{1,9},{5,13},{9,1},{13,5},{2,10},{6,14},... | collective-permute-start | bytes 3145736 | tf_op jit(solution)/shard_map/ppermute | solution.py:27
  12.2 38.5 %collective-permute-done.3 = bf16[32,8,2048]{2,1,0:T(8,128)(2,1)} collective-permute-done((bf16[32,8,2048]{2,1,0:T(8,128)(2,1)}, bf16[32,8,2048]{2,1,0:T(8,128)(2,1)}, u32[]{:S(2)}, u32[]{:S(2)}) %collective-permute-start.3) | collective-permute-done | bytes 1048608 | tf_op jit(solution)/shard_map/ppermute | solution.py:27
  64.7 18.2 %collective-permute-done.5 = bf16[2,16,8,2048]{3,2,1,0:T(8,128)(2,1)S(1)} collective-permute-done((bf16[2,16,8,2048]{3,2,1,0:T(8,128)(2,1)S(1)}, bf16[2,16,8,2048]{3,2,1,0:T(8,128)(2,1)S(1)}, u32[]{:S(2)}, u32[]{:S(2)}) %collective-permute-start.5) | collective-permute-done | bytes 1048608 | tf_op jit(solution)/shard_map/ppermute | solution.py:17
  82.8 22.5 %collective-permute-done.2 = bf16[2,16,8,2048]{3,2,1,0:T(8,128)(2,1)S(1)} collective-permute-done((bf16[2,16,8,2048]{3,2,1,0:T(8,128)(2,1)S(1)}, bf16[2,16,8,2048]{3,2,1,0:T(8,128)(2,1)S(1)}, u32[]{:S(2)}, u32[]{:S(2)}) %collective-permute-start.2) | collective-permute-done | bytes 1048608 | tf_op jit(solution)/shard_map/ppermute | solution.py:17
  108.9 2.8 %reshape_reshape.12 = bf16[128,64,128]{2,1,0:T(8,128)(2,1)} reshape(bf16[16,8,4,2048]{3,2,1,0:T(4,128)(2,1)S(1)} %copy.36) | data formatting | bytes 4194304 | tf_op jit(solution)/shard_map/reshape;reshape | solution.py:63
  111.7 3.1 %copy.38 = bf16[128,64,128]{2,0,1:T(8,128)(2,1)S(1)} copy(bf16[128,64,128]{2,1,0:T(8,128)(2,1)} %reshape_reshape.12) | data formatting | bytes 4194304 | tf_op jit(solution)/shard_map/reshape;reshape | solution.py:63
  115.0 3.1 %copy.40 = bf16[16,8,4,2048]{3,2,1,0:T(4,128)(2,1)} copy(bf16[16,8,4,2048]{3,1,0,2:T(8,128)(2,1)S(1)} %maximum_bitcast_fusion.1) | data formatting | bytes 4194304 | tf_op jit(solution)/shard_map/transpose | solution.py:10
  118.2 4.4 %reshape_reshape.13 = bf16[128,64,128]{2,1,0:T(8,128)(2,1)} reshape(bf16[16,8,4,2048]{3,2,1,0:T(4,128)(2,1)} %copy.40) | data formatting | bytes 4194304 | tf_op jit(solution)/shard_map/reshape;reshape | solution.py:63
  122.5 4.4 %copy.42 = bf16[128,64,128]{2,0,1:T(8,128)(2,1)} copy(bf16[128,64,128]{2,1,0:T(8,128)(2,1)} %reshape_reshape.13) | data formatting | bytes 4194304 | tf_op jit(solution)/shard_map/reshape;reshape | solution.py:63
  127.9 21.6 %collective-permute-done.7 = bf16[2,16,8,2048]{3,2,1,0:T(8,128)(2,1)} collective-permute-done((bf16[2,16,8,2048]{3,2,1,0:T(8,128)(2,1)}, bf16[2,16,8,2048]{3,2,1,0:T(8,128)(2,1)}, u32[]{:S(2)}, u32[]{:S(2)}) %collective-permute-start.7) | collective-permute-done | bytes 1048608 | tf_op jit(solution)/shard_map/ppermute | solution.py:17
  149.5 3.2 %broadcast_select_fusion.1 = (bf16[2,16,8,2048]{3,2,1,0:T(8,128)(2,1)}, bf16[2,16,8,2048]{3,2,1,0:T(8,128)(2,1)}, bf16[2,16,8,2048]{3,2,1,0:T(8,128)(2,1)S(1)}, bf16[2,16,8,2048]{3,2,1,0:T(8,128)(2,1)S(1)}) fusion(bf16[2,16,8,2048]{3,2,1,0:T(8,128)(2,1)} %collective-permute-done.9, pred[]{:T(512)S(6)} %eq.4, ...), kind=kLoop, calls=%fused_computation.57 | loop fusion | flops 3145728 | bytes 8388609 | tf_op jit(solution)/shard_map/jit(_where)/select_n | solution.py:19
  152.9 3.1 %copy.44 = bf16[16,8,4,2048]{3,2,1,0:T(4,128)(2,1)} copy(bf16[16,8,4,2048]{3,1,0,2:T(8,128)(2,1)S(1)} %maximum_bitcast_fusion.2) | data formatting | bytes 4194304 | tf_op jit(solution)/shard_map/transpose | solution.py:10
  156.0 4.4 %reshape_reshape.14 = bf16[128,64,128]{2,1,0:T(8,128)(2,1)} reshape(bf16[16,8,4,2048]{3,2,1,0:T(4,128)(2,1)} %copy.44) | data formatting | bytes 4194304 | tf_op jit(solution)/shard_map/reshape;reshape | solution.py:63
  160.4 4.4 %copy.46 = bf16[128,64,128]{2,0,1:T(8,128)(2,1)} copy(bf16[128,64,128]{2,1,0:T(8,128)(2,1)} %reshape_reshape.14) | data formatting | bytes 4194304 | tf_op jit(solution)/shard_map/reshape;reshape | solution.py:63
  165.0 3.1 %copy.48 = bf16[16,8,4,2048]{3,2,1,0:T(4,128)(2,1)} copy(bf16[16,8,4,2048]{3,1,0,2:T(8,128)(2,1)S(1)} %maximum_bitcast_fusion.3) | data formatting | bytes 4194304 | tf_op jit(solution)/shard_map/transpose | solution.py:10
  168.2 4.4 %reshape_reshape.15 = bf16[128,64,128]{2,1,0:T(8,128)(2,1)} reshape(bf16[16,8,4,2048]{3,2,1,0:T(4,128)(2,1)} %copy.48) | data formatting | bytes 4194304 | tf_op jit(solution)/shard_map/reshape;reshape | solution.py:63
  172.6 4.3 %copy.50 = bf16[128,64,128]{2,0,1:T(8,128)(2,1)} copy(bf16[128,64,128]{2,1,0:T(8,128)(2,1)} %reshape_reshape.15) | data formatting | bytes 4194304 | tf_op jit(solution)/shard_map/reshape;reshape | solution.py:63
  179.1 3.9 %gather_fusion.1 = bf16[64,128,128]{2,1,0:T(8,128)(2,1)} fusion(bf16[128,64,128]{2,0,1:T(8,128)(2,1)} %copy.42, s32[1024]{0:T(1024)S(1)} %pad_clamp_fusion.2), kind=kCustom, calls=%fused_computation.1.clone | custom fusion | bytes 4194560 | tf_op jit(solution)/shard_map/jit(_take)/gather | solution.py:64
  185.2 2.5 %gather_fusion.3 = bf16[64,128,128]{2,1,0:T(8,128)(2,1)S(1)} fusion(bf16[128,64,128]{2,0,1:T(8,128)(2,1)} %copy.50, s32[1024]{0:T(1024)S(1)} %pad_clamp_fusion), kind=kCustom, calls=%fused_computation.3.clone | custom fusion | bytes 4194560 | tf_op jit(solution)/shard_map/jit(_take)/gather | solution.py:64
  187.8 3.1 %fusion.28 = f32[16,128,128]{2,1,0:T(8,128)S(1)} fusion(bf16[4,1,16,4,128,128]{5,4,3,2,1,0:T(8,128)(2,1)} %param.23, bf16[16,4,128,128]{3,2,1,0:T(8,128)(2,1)} %bitcast.149, pred[16,4]{1,0:T(8,128)(4,1)S(1)} %copy.35), kind=kOutput, calls=%fused_computation.40 | convolution fusion | flops 269484032 | bytes 5242944 | tf_op jit(solution)/shard_map/rjkc,jkcd->rjd/dot_general | solution.py:65
  190.9 2.5 %fusion.63 = f32[16,128,128]{2,1,0:T(8,128)S(1)} fusion(f32[16,128,128]{2,1,0:T(8,128)S(1)} %fusion.28, bf16[4,1,16,4,128,128]{5,4,3,2,1,0:T(8,128)(2,1)} %param.23, bf16[16,4,128,128]{3,2,1,0:T(8,128)(2,1)S(1)} %bitcast.150, pred[16,4]{1,0:T(8,128)(4,1)S(1)} %copy.39), kind=kOutput, calls=%fused_computation.47 | convolution fusion | flops 269746176 | bytes 6291520 | tf_op jit(solution)/shard_map/rjkc,jkcd->rjd/dot_general | solution.py:65
  193.5 2.4 %fusion.58 = f32[16,128,128]{2,1,0:T(8,128)S(1)} fusion(f32[16,128,128]{2,1,0:T(8,128)S(1)} %fusion.63, bf16[4,1,16,4,128,128]{5,4,3,2,1,0:T(8,128)(2,1)} %param.23, bf16[16,4,128,128]{3,2,1,0:T(8,128)(2,1)S(1)} %bitcast.148, pred[16,4]{1,0:T(8,128)(4,1)S(1)} %copy.43), kind=kOutput, calls=%fused_computation.46 | convolution fusion | flops 269746176 | bytes 6291520 | tf_op jit(solution)/shard_map/rjkc,jkcd->rjd/dot_general | solution.py:65
  195.9 2.4 %fusion.53 = f32[128,16,128]{2,0,1:T(8,128)S(1)} fusion(f32[16,128,128]{2,1,0:T(8,128)S(1)} %fusion.58, bf16[4,1,16,4,128,128]{5,4,3,2,1,0:T(8,128)(2,1)} %param.23, bf16[16,4,128,128]{3,2,1,0:T(8,128)(2,1)S(1)} %bitcast.147, pred[16,4]{1,0:T(8,128)(4,1)S(1)} %copy.47), kind=kOutput, calls=%fused_computation.45 | convolution fusion | flops 269746176 | bytes 6291520 | tf_op jit(solution)/shard_map/rjkc,jkcd->rjd/dot_general | solution.py:65
  199.2 15.5 %while.18 = (s32[]{:T(128)}, f32[8,2048]{1,0:T(8,128)S(1)}, f32[8,2048]{1,0:T(8,128)S(1)}, bf16[16,8,2048]{2,1,0:T(8,128)(2,1)S(1)}, f32[2048]{0:T(1024)S(1)}, /...) while((s32[]{:T(128)}, f32[8,2048]{1,0:T(8,128)S(1)}, ...), condition=%wide.region_1.3_spmd, body=%wide.region_0.2_spmd.sunk | while | flops 180227 | bytes 581777 | solution.py:40
  (125 shorter events, 42.5 us)
Async XLA Ops:
  0.6 50.2 %collective-permute-start.3 = (bf16[32,8,2048]{2,1,0:T(8,128)(2,1)}, bf16[32,8,2048]{2,1,0:T(8,128)(2,1)}, u32[]{:S(2)}, u32[]{:S(2)}) collective-permute-start(bf16[32,8,2048]{2,1,0:T(8,128)(2,1)} %param.15), channel_id=1, source_target_pairs={{0,8},{4,12},{8,0},{12,4},{1,9},{5,13},{9,1},{13,5},{2,10},{6,14},... | collective-permute-start | bytes 3145736 | tf_op jit(solution)/shard_map/ppermute | solution.py:27
  4.7 50.6 %collective-permute-start = (bf16[32,8,2048]{2,1,0:T(8,128)(2,1)}, bf16[32,8,2048]{2,1,0:T(8,128)(2,1)S(1)}, u32[]{:S(2)}, u32[]{:S(2)}) collective-permute-start(bf16[32,8,2048]{2,1,0:T(8,128)(2,1)} %param.15), channel_id=1, source_target_pairs={{0,4},{4,0},{8,12},{12,8},{1,5},{5,1},{9,13},{13,9},{2,6},{6,2},{1... | collective-permute-start | bytes 3145736 | tf_op jit(solution)/shard_map/ppermute | solution.py:27
  52.1 4.5 %collective-permute-start.4 = (bf16[1,16,8,2048]{3,2,1,0:T(8,128)(2,1)S(1)}, bf16[1,16,8,2048]{3,2,1,0:T(8,128)(2,1)S(1)}, u32[]{:S(2)}, u32[]{:S(2)}) collective-permute-start(bf16[1,16,8,2048]{3,2,1,0:T(8,128)(2,1)S(1)} %get-tuple-element.240), channel_id=1, source_target_pairs={{0,1},{1,0},{2,3},{3,2},{4,5},{5,4},{6,7},{7,6},{8,9},{9,8},{10,11... | collective-permute-start | bytes 1572872 | tf_op jit(solution)/shard_map/ppermute | solution.py:17
  55.5 2.9 %collective-permute-start.1 = (bf16[1,16,8,2048]{3,2,1,0:T(8,128)(2,1)S(1)}, bf16[1,16,8,2048]{3,2,1,0:T(8,128)(2,1)S(1)}, u32[]{:S(2)}, u32[]{:S(2)}) collective-permute-start(bf16[1,16,8,2048]{3,2,1,0:T(8,128)(2,1)S(1)} %get-tuple-element.244), channel_id=1, source_target_pairs={{0,1},{1,0},{2,3},{3,2},{4,5},{5,4},{6,7},{7,6},{8,9},{9,8},{10,11... | collective-permute-start | bytes 1572872 | tf_op jit(solution)/shard_map/ppermute | solution.py:17
  56.1 3.3 %collective-permute-start.8 = (bf16[1,16,8,2048]{3,2,1,0:T(8,128)(2,1)S(1)}, bf16[1,16,8,2048]{3,2,1,0:T(8,128)(2,1)S(1)}, u32[]{:S(2)}, u32[]{:S(2)}) collective-permute-start(bf16[1,16,8,2048]{3,2,1,0:T(8,128)(2,1)S(1)} %get-tuple-element.239), channel_id=1, source_target_pairs={{0,1},{1,0},{2,3},{3,2},{4,5},{5,4},{6,7},{7,6},{8,9},{9,8},{10,11... | collective-permute-start | bytes 1572872 | tf_op jit(solution)/shard_map/ppermute | solution.py:17
  56.1 5.6 %collective-permute-start.6 = (bf16[1,16,8,2048]{3,2,1,0:T(8,128)(2,1)S(1)}, bf16[1,16,8,2048]{3,2,1,0:T(8,128)(2,1)S(1)}, u32[]{:S(2)}, u32[]{:S(2)}) collective-permute-start(bf16[1,16,8,2048]{3,2,1,0:T(8,128)(2,1)S(1)} %get-tuple-element.243), channel_id=1, source_target_pairs={{0,1},{1,0},{2,3},{3,2},{4,5},{5,4},{6,7},{7,6},{8,9},{9,8},{10,11... | collective-permute-start | bytes 1572872 | tf_op jit(solution)/shard_map/ppermute | solution.py:17
  56.8 26.1 %collective-permute-start.5 = (bf16[2,16,8,2048]{3,2,1,0:T(8,128)(2,1)S(1)}, bf16[2,16,8,2048]{3,2,1,0:T(8,128)(2,1)S(1)}, u32[]{:S(2)}, u32[]{:S(2)}) collective-permute-start(bf16[2,16,8,2048]{3,2,1,0:T(8,128)(2,1)S(1)} %pad_maximum_fusion.1), channel_id=1, source_target_pairs={{0,2},{1,3},{2,0},{3,1},{4,6},{5,7},{6,4},{7,5},{8,10},{9,11},{10,... | collective-permute-start | bytes 3145736 | tf_op jit(solution)/shard_map/ppermute | solution.py:17
  58.5 46.8 %collective-permute-start.2 = (bf16[2,16,8,2048]{3,2,1,0:T(8,128)(2,1)S(1)}, bf16[2,16,8,2048]{3,2,1,0:T(8,128)(2,1)S(1)}, u32[]{:S(2)}, u32[]{:S(2)}) collective-permute-start(bf16[2,16,8,2048]{3,2,1,0:T(8,128)(2,1)S(1)} %pad_maximum_fusion), channel_id=1, source_target_pairs={{0,2},{1,3},{2,0},{3,1},{4,6},{5,7},{6,4},{7,5},{8,10},{9,11},{10,... | collective-permute-start | bytes 3145736 | tf_op jit(solution)/shard_map/ppermute | solution.py:17
  60.5 67.3 %collective-permute-start.9 = (bf16[2,16,8,2048]{3,2,1,0:T(8,128)(2,1)}, bf16[2,16,8,2048]{3,2,1,0:T(8,128)(2,1)}, u32[]{:S(2)}, u32[]{:S(2)}) collective-permute-start(bf16[2,16,8,2048]{3,2,1,0:T(8,128)(2,1)} %pad_maximum_fusion.3), channel_id=1, source_target_pairs={{0,2},{1,3},{2,0},{3,1},{4,6},{5,7},{6,4},{7,5},{8,10},{9,11},{10,... | collective-permute-start | bytes 3145736 | tf_op jit(solution)/shard_map/ppermute | solution.py:17
  61.9 2.0 copy-start.5
  63.9 85.6 %collective-permute-start.7 = (bf16[2,16,8,2048]{3,2,1,0:T(8,128)(2,1)}, bf16[2,16,8,2048]{3,2,1,0:T(8,128)(2,1)}, u32[]{:S(2)}, u32[]{:S(2)}) collective-permute-start(bf16[2,16,8,2048]{3,2,1,0:T(8,128)(2,1)} %pad_maximum_fusion.2), channel_id=1, source_target_pairs={{0,2},{1,3},{2,0},{3,1},{4,6},{5,7},{6,4},{7,5},{8,10},{9,11},{10,... | collective-permute-start | bytes 3145736 | tf_op jit(solution)/shard_map/ppermute | solution.py:17
  111.7 3.1 %copy-start.9 = (bf16[2,16,8,2048]{3,2,1,0:T(8,128)(2,1)S(1)}, bf16[2,16,8,2048]{3,2,1,0:T(8,128)(2,1)}, u32[]{:S(2)}) copy-start(bf16[2,16,8,2048]{3,2,1,0:T(8,128)(2,1)} %get-tuple-element.233) | copy-start | bytes 3145732
  111.7 3.1 %copy-start.10 = (bf16[2,16,8,2048]{3,2,1,0:T(8,128)(2,1)S(1)}, bf16[2,16,8,2048]{3,2,1,0:T(8,128)(2,1)}, u32[]{:S(2)}) copy-start(bf16[2,16,8,2048]{3,2,1,0:T(8,128)(2,1)} %get-tuple-element.234) | copy-start | bytes 3145732
  122.5 26.9 %copy-start.4 = (bf16[1,16,8,2048]{3,2,1,0:T(8,128)(2,1)S(1)}, bf16[1,16,8,2048]{3,2,1,0:T(8,128)(2,1)}, u32[]{:S(2)}) copy-start(bf16[1,16,8,2048]{3,2,1,0:T(8,128)(2,1)} %copy-done.3) | copy-start | bytes 1572868
  122.5 26.9 %copy-start.6 = (bf16[1,16,8,2048]{3,2,1,0:T(8,128)(2,1)S(1)}, bf16[1,16,8,2048]{3,2,1,0:T(8,128)(2,1)}, u32[]{:S(2)}) copy-start(bf16[1,16,8,2048]{3,2,1,0:T(8,128)(2,1)} %copy-done.5) | copy-start | bytes 1572868
  160.4 4.4 %copy-start.7 = (bf16[2,16,8,2048]{3,2,1,0:T(8,128)(2,1)S(1)}, bf16[2,16,8,2048]{3,2,1,0:T(8,128)(2,1)}, u32[]{:S(2)}) copy-start(bf16[2,16,8,2048]{3,2,1,0:T(8,128)(2,1)} %get-tuple-element.229) | copy-start | bytes 3145732
  160.4 4.4 %copy-start.8 = (bf16[2,16,8,2048]{3,2,1,0:T(8,128)(2,1)S(1)}, bf16[2,16,8,2048]{3,2,1,0:T(8,128)(2,1)}, u32[]{:S(2)}) copy-start(bf16[2,16,8,2048]{3,2,1,0:T(8,128)(2,1)} %get-tuple-element.230) | copy-start | bytes 3145732
  179.1 3.9 %copy-start = (bf16[128,64,128]{2,0,1:T(8,128)(2,1)S(1)}, bf16[128,64,128]{2,0,1:T(8,128)(2,1)}, u32[]{:S(2)}) copy-start(bf16[128,64,128]{2,0,1:T(8,128)(2,1)} %copy.46) | copy-start | bytes 6291460
  187.8 3.1 %copy-start.14 = (bf16[64,128,128]{2,1,0:T(8,128)(2,1)S(1)}, bf16[64,128,128]{2,1,0:T(8,128)(2,1)}, u32[]{:S(2)}) copy-start(bf16[64,128,128]{2,1,0:T(8,128)(2,1)} %gather_fusion.1) | copy-start | bytes 6291460
  190.9 2.6 %copy-start.13 = (bf16[64,128,128]{2,1,0:T(8,128)(2,1)S(1)}, bf16[64,128,128]{2,1,0:T(8,128)(2,1)}, u32[]{:S(2)}) copy-start(bf16[64,128,128]{2,1,0:T(8,128)(2,1)} %gather_fusion.2) | copy-start | bytes 6291460
  198.3 0.9 copy-start.2
  198.3 0.9 copy-start.12
  198.3 0.9 copy-start.16
  198.3 0.9 copy-start.17
  (5 other events, 3.8 us)
